TPU v7x, 32 devices: a whole 2x2x4 slice. The times are simulated.
32 devices in a mesh: groups: 2 (over y), blk: 4 (over z), cls: 4 (over x, core).
Axes of the slice: x: 2, y: 2, z: 4, core: 2. Of those that a mesh axis runs over, the one named last changes fastest.
Arguments:
- particles: bfloat16 [64, 4096], P(('groups', 'blk')), parts along dimension 0
- references: bfloat16 [4, 400, 4096], P('blk', ('groups', 'cls')), parts along dimension 1
- ctf_table: float32 [32, 2048], P('groups'), parts along dimension 0, may hold values from 0.05 to 1
- spectral_reg: float32 [4096], P('groups'), parts along dimension 0, may hold values from 0.002 to 0.02
- defocus_bin: int32 [64], P(('groups', 'blk')), parts along dimension 0, may hold values from 0 to 15
- group_counts: int32 [32], P(('groups', 'blk')), parts along dimension 0, may hold values from 0 to 8, as said below
- group_scale: float32 [32], P(('groups', 'blk')), parts along dimension 0, may hold values from 0.5 to 2
Outputs:
- class_average: float32 [4, 400, 4096], P('blk', ('groups', 'cls')), parts along dimension 1
- log_evidence: float32 [64], P(('groups', 'blk')), parts along dimension 0
There are 2 independent parts, one for each index of `groups`. A program takes and returns all parts, laid end to end along the dimension named above; each array names one. Nothing has to cross between parts.
Inputs may be any that keep to these rules, and one draw needn't show every extreme that they name: `group_counts`: the 4 groups of one block of 8 slots hold at most 8 particles together, filling the block's first slots; in every draw some single group holds exactly 8.
All inputs are finite; a program needn't handle non-finite values.
Results may differ from a plain program's by a relative error of at most 0.013.
Values may be sent and summed in bfloat16 or wider, within the bound.
No kernel may reach another device: no remote copies, remote signals or barrier semaphores. Data moves between devices by JAX's collectives and lax.ppermute only.
A program may use at most 64 MiB of HBM per device.

v0:
```python
import math
import jax
import jax.numpy as jnp
from jax import lax
from jax.sharding import PartitionSpec as P

KX = 32
KY = 64
IMG = 128
SIDE = 4
BINS = 16
HIGHEST = lax.Precision.HIGHEST


def combined_all(value, axis, join):
    pieces = jax.tree.map(lambda part: lax.all_gather(part, axis), value)
    head = jax.tree.map(lambda part: part[0], pieces)
    tail = jax.tree.map(lambda part: part[1:], pieces)
    running, _ = lax.scan(lambda running, section: (join(running, section), None), head, tail)
    return running


def phase_tables():
    column = jnp.arange(KX * KY, dtype=jnp.int32)
    freq_x = (column % KX).astype(jnp.float32)
    freq_y = (column // KX - KY // 2).astype(jnp.float32)
    offsets = jnp.arange(SIDE, dtype=jnp.float32) - (SIDE - 1) / 2.0
    shift_x = jnp.tile(offsets, SIDE)
    shift_y = jnp.repeat(offsets, SIDE)
    phases = (
        2.0
        * math.pi
        / IMG
        * (shift_x[:, None] * freq_x[None, :] + shift_y[:, None] * freq_y[None, :])
    )
    return (jnp.cos(phases), jnp.sin(phases))


def bin_matrix(bin_values):
    return (bin_values[:, None] == jnp.arange(BINS, dtype=jnp.float32)[None, :]).astype(jnp.float32)


def slot_weights(group_sizes, scale_rows, slots):
    group_ends = jnp.cumsum(group_sizes, axis=1)
    group_starts = group_ends - group_sizes
    slot_index = jnp.arange(slots, dtype=jnp.int32)
    membership = (
        (slot_index[None, :, None] >= group_starts[:, None, :])
        & (slot_index[None, :, None] < group_ends[:, None, :])
    ).astype(jnp.float32)
    gain_rows = jnp.sum(membership * scale_rows[:, None, :], axis=2)
    live_mask = jnp.sum(membership, axis=2)
    return (gain_rows.reshape(-1), live_mask.reshape(-1))


def shifted_rows(images, ctf_rows, cosine_table, sine_table):
    half_width = ctf_rows.shape[1]
    real_part = images[:, :half_width].astype(jnp.float32)[:, None, :]
    imag_part = images[:, half_width:].astype(jnp.float32)[:, None, :]
    ctf_wide = ctf_rows[:, None, :]
    new_real = (real_part * cosine_table + imag_part * sine_table) * ctf_wide
    new_imag = (imag_part * cosine_table - real_part * sine_table) * ctf_wide
    joined = jnp.concatenate([new_real, new_imag], axis=2).astype(jnp.bfloat16)
    return joined.reshape(images.shape[0] * cosine_table.shape[0], 2 * half_width)


def tile_norms(ref_rows, ctf_square):
    half_width = ctf_square.shape[1]
    values = ref_rows.astype(jnp.float32)
    power_sum = (
        values[:, :half_width] * values[:, :half_width]
        + values[:, half_width:] * values[:, half_width:]
    )
    return lax.dot_general(ctf_square, power_sum, (((1,), (1,)), ((), ())), precision=HIGHEST)


def tile_scores(shifted, ref_rows, norms, gain_rows, bin_rows):
    count_here = gain_rows.shape[0]
    products = lax.dot_general(
        shifted, ref_rows, (((1,), (1,)), ((), ())), preferred_element_type=jnp.float32
    )
    products = products.reshape(count_here, shifted.shape[0] // count_here, ref_rows.shape[0])
    norm_term = jnp.dot(bin_rows, norms, precision=HIGHEST)
    return (
        gain_rows[:, None, None] * products
        - 0.5 * (gain_rows * gain_rows)[:, None, None] * norm_term[:, None, :]
    )


def combine_stats(former, latter):
    new_peak = jnp.maximum(former[0], latter[0])
    return (
        new_peak,
        former[1] * jnp.exp(former[0] - new_peak) + latter[1] * jnp.exp(latter[0] - new_peak),
    )


def accumulate(running, shifted, scores, gain_rows, bin_rows, live_mask, peak_score, totals):
    weights = (
        jnp.exp(scores - peak_score[:, None, None])
        / totals[:, None, None]
        * live_mask[:, None, None]
    )
    scaled = (weights * gain_rows[:, None, None]).astype(jnp.bfloat16).reshape(shifted.shape[0], -1)
    numerator = running[0] + lax.dot_general(
        scaled, shifted, (((0,), (0,)), ((), ())), preferred_element_type=jnp.float32
    )
    summed = jnp.sum(weights, axis=1) * (gain_rows * gain_rows)[:, None]
    bin_weight = running[1] + lax.dot_general(
        summed, bin_rows, (((0,), (0,)), ((), ())), precision=HIGHEST
    )
    return (numerator, bin_weight)


def per_device(
    particles, references, ctf_table, spectral_reg, defocus_bin, group_counts, group_scale
):
    cosine_table, sine_table = phase_tables()
    ctf_square = ctf_table * ctf_table
    batch_size = particles.shape[0]
    gain_rows, live_mask = slot_weights(
        group_counts.reshape(1, -1), group_scale.reshape(1, -1), batch_size
    )
    bin_values = defocus_bin.astype(jnp.float32)
    ref_tile = references[0]
    own_norms = tile_norms(ref_tile, ctf_square)
    classes_here = ref_tile.shape[0]
    zero_sums = (
        jnp.zeros((classes_here, ref_tile.shape[1]), jnp.float32),
        jnp.zeros((classes_here, ctf_table.shape[0]), jnp.float32),
    )

    def batch_rows(images, bins_part):
        bin_rows = bin_matrix(bins_part)
        ctf_rows = jnp.dot(bin_rows, ctf_table, precision=HIGHEST)
        return (shifted_rows(images, ctf_rows, cosine_table, sine_table), bin_rows)

    everyone = lax.all_gather(particles, "blk", axis=0, tiled=True)
    gain_all, bins_all, live_all = (
        lax.all_gather(gain_rows, "blk", axis=0, tiled=True),
        lax.all_gather(bin_values, "blk", axis=0, tiled=True),
        lax.all_gather(live_mask, "blk", axis=0, tiled=True),
    )
    whole_count = everyone.shape[0]
    block_size = math.gcd(whole_count, 32)
    block_count = whole_count // block_size

    def block_inputs(block_index):
        offset = block_index * block_size
        images = lax.dynamic_slice_in_dim(everyone, offset, block_size)
        gains_part = lax.dynamic_slice_in_dim(gain_all, offset, block_size)
        shifted, bin_rows = batch_rows(
            images, lax.dynamic_slice_in_dim(bins_all, offset, block_size)
        )
        return (offset, shifted, bin_rows, gains_part)

    def block_scores(block_index):
        offset, shifted, bin_rows, gains_part = block_inputs(block_index)
        return tile_scores(shifted, ref_tile, own_norms, gains_part, bin_rows)

    all_scores = lax.map(block_scores, jnp.arange(block_count, dtype=jnp.int32))
    all_scores = all_scores.reshape(whole_count, cosine_table.shape[0], classes_here)
    flattened = all_scores.reshape(whole_count, -1)
    peak_all = jnp.max(flattened, axis=1)
    totals_all = jnp.sum(jnp.exp(flattened - peak_all[:, None]), axis=1)
    peak_all, totals_all = combined_all((peak_all, totals_all), ("blk", "cls"), combine_stats)

    def block_sums(block_index, running):
        offset, shifted, bin_rows, gains_part = block_inputs(block_index)
        scores = lax.dynamic_slice_in_dim(all_scores, offset, block_size)
        live_part = lax.dynamic_slice_in_dim(live_all, offset, block_size)
        peak_part = lax.dynamic_slice_in_dim(peak_all, offset, block_size)
        totals_part = lax.dynamic_slice_in_dim(totals_all, offset, block_size)
        return accumulate(
            running, shifted, scores, gains_part, bin_rows, live_part, peak_part, totals_part
        )

    numerator, bin_weight = lax.fori_loop(0, block_count, block_sums, zero_sums)
    own_offset = lax.axis_index("blk") * batch_size
    peak_score = lax.dynamic_slice_in_dim(peak_all, own_offset, batch_size)
    totals = lax.dynamic_slice_in_dim(totals_all, own_offset, batch_size)
    log_evidence = jnp.where(live_mask > 0.5, peak_score + jnp.log(totals), 0.0)
    denominator = jnp.dot(bin_weight, ctf_square, precision=HIGHEST)
    denominator = (
        jnp.concatenate([denominator, denominator], axis=1)
        + jnp.concatenate([spectral_reg, spectral_reg])[None, :]
    )
    class_average = (numerator / denominator)[None]
    return (class_average, log_evidence)


def solution(mesh):
    placed = (
        P(("groups", "blk"), None),
        P("blk", ("groups", "cls"), None),
        P("groups", None),
        P("groups"),
        P(("groups", "blk")),
        P(("groups", "blk")),
        P(("groups", "blk")),
    )
    return jax.shard_map(
        per_device,
        mesh=mesh,
        in_specs=placed,
        out_specs=(P("blk", ("groups", "cls"), None), P(("groups", "blk"))),
        check_vma=False,
    )
```

profile of v0, /device:TPU:0, one launch (start us, length us, event | category | flops | bytes accessed | tf_op | source)
XLA Modules:
  0.0 79.3 jit_solution(13035143194727210498)
XLA Ops:
  0.7 1.3 %dynamic-slice.2 = u32[1]{0:T(128)} dynamic-slice(u32[32]{0:T(128)} %constant.106, u32[]{:T(128)S(6)} %add.107), dynamic_slice_sizes={1} | dynamic-slice | bytes 12
  2.6 1.2 %dynamic-slice = u32[1]{0:T(128)} dynamic-slice(u32[32]{0:T(128)} %constant.96, u32[]{:T(128)S(6)} %add.107), dynamic_slice_sizes={1} | dynamic-slice | bytes 12
  4.5 0.8 %reduce-window.7 = s32[4,1]{0,1:T(1,128)S(1)} reduce-window(s32[4,1]{0,1:T(1,128)} %bitcast.39, s32[]{:T(128)} %copy.31), window={size=4x1 pad=3_0x0_0}, to_apply=%region_0.1 | reduce-window | flops 12 | bytes 36 | tf_op jit(solution)/shard_map/reduce-window.2
  5.3 0.7 bitcast_subtract_fusion
  6.0 0.7 select_reduce_fusion
  6.7 0.2 dynamic-update-slice.4
  7.0 0.7 convert_dynamic-update-slice_fusion
  7.7 0.2 dynamic-update-slice
  7.9 13.4 %all-reduce.6 = (f32[32]{0:T(128)S(1)}, f32[32]{0:T(128)S(1)}, f32[32]{0:T(128)S(1)}) all-reduce(f32[32]{0:T(128)S(1)} %convert_dynamic-update-slice_fusion, f32[32]{0:T(128)S(1)} %dynamic-update-slice.4, f32[32]{0:T(128)S(1)} %dynamic-update-slice), channel_id=1, replica_groups=mesh['groups'=2,'blk'=4,'cls'=4] {'blk'}, use_global_device_ids=true, to_apply=%add.1 | all-reduce | flops 96 | bytes 768
  21.4 0.1 mul.359
  21.5 0.1 mul.355
  21.6 0.8 pad_maximum_fusion.7
  22.4 0.5 fusion.15
  22.9 1.2 %fusion.22 = f32[32,2048]{1,0:T(8,128)S(1)} fusion(f32[16,2048]{1,0:T(8,128)} %param.11, f32[32]{0:T(128)S(1)} %get-tuple-element.122), kind=kOutput, calls=%fused_computation.40 | convolution fusion | flops 12583424 | bytes 393344 | tf_op jit(solution)/shard_map/while/body/eval_jaxpr/dot_general | solution.py:135
  24.2 14.1 %all_gather.25 = bf16[32,4096]{1,0:T(8,128)(2,1)S(1)} all-gather(bf16[8,4096]{1,0:T(8,128)(2,1)} %param.9), channel_id=1, replica_groups=mesh['groups'=2,'blk'=4,'cls'=4] {'blk'}, dimensions={0}, use_global_device_ids=true | all-gather | bytes 327680 | tf_op jit(solution)/shard_map/all_gather | solution.py:138
  38.4 0.5 fusion.11
  38.8 0.2 convolution_multiply_fusion
  39.1 1.5 %multiply_convert_fusion.1 = (bf16[32,16,2048]{2,1,0:T(8,128)(2,1)S(1)}, bf16[32,16,2048]{2,1,0:T(8,128)(2,1)S(1)}) fusion(f32[32,2048]{1,0:T(8,128)S(1)} %fusion.22, f32[16,2048]{1,0:T(8,128)S(1)} %get-tuple-element.132, f32[32,2048]{1,0:T(8,128)S(1)} %get-tuple-element.130, f32[16,2048]{1,0:T(8,128)S(1)} %get-tuple-element.131, ...), kind=kLoop, calls=%fused_computation.12 | loop fusion | flops 10485760 | bytes 5242880 | tf_op jit(solution)/shard_map/convert
  40.6 1.4 %fusion.40 = (f32[32]{0:T(128)S(1)}, f32[32,16,50]{2,1,0:T(8,128)S(1)}) fusion(f32[32,50]{1,0:T(8,128)S(1)} %convolution_multiply_fusion, bf16[1,50,4096]{2,1,0:T(8,128)(2,1)S(1)} %copy-done.2, bf16[32,16,2048]{2,1,0:T(8,128)(2,1)S(1)} %get-tuple-element.128, bf16[32,16,2048]{2,1,0:T(8,128)(2,1)S(1)} %get-tuple-element.127, f32[32]{0:T(128)S(1)} %get-tuple-element.124), kind=kOutput, calls=%fused_computation.71 | convolution fusion | flops 218180576 | bytes 4712960 | tf_op jit(solution)/shard_map/while/body/eval_jaxpr/dot_general | solution.py:79
  42.1 0.2 dynamic-update-slice.2
  42.3 0.5 exponential_reduce_fusion
  42.8 0.2 dynamic-update-slice.3
  43.0 29.5 %all-reduce.5 = (f32[512]{0:T(512)S(1)}, f32[512]{0:T(512)S(1)}) all-reduce(f32[512]{0:T(512)S(1)} %dynamic-update-slice.2, f32[512]{0:T(512)S(1)} %dynamic-update-slice.3), channel_id=2, replica_groups=mesh['groups'=2,'blk'=4,'cls'=4] {'blk','cls'}, use_global_device_ids=true, to_apply=%add.2 | all-reduce | flops 1024 | bytes 8192
  72.7 0.1 reshape.391
  72.7 0.1 reshape.390
  72.8 0.6 while.2
  73.4 0.6 compare_select_fusion
  74.0 0.2 fusion.38
  74.2 0.3 fusion.20
  74.5 0.5 fusion.17
  75.0 2.6 %fusion.6 = f32[1,50,4096]{2,1,0:T(8,128)S(1)} fusion(bf16[32,16,2048]{2,1,0:T(8,128)(2,1)} %copy-done, bf16[32,16,2048]{2,1,0:T(8,128)(2,1)S(1)} %get-tuple-element.127, f32[50,2048]{1,0:T(8,128)S(1)} %fusion.17, f32[4096]{0:T(1024)S(1)} %pad_maximum_fusion.7, f32[32]{0:T(128)S(1)} %get-tuple-element.124, f32[32,16,50]{2,1,0:T(8,128)S(1)} %get-tuple-element.136, ...), kind=kOutput, calls=%fused_computation.9 | convolution fusion | flops 218846208 | bytes 5542400 | tf_op jit(solution)/shard_map/while/body/eval_jaxpr/dot_general | solution.py:105
  77.6 1.7 %copy.14 = f32[1,50,4096]{2,0,1:T(1,128)} copy(f32[1,50,4096]{2,1,0:T(8,128)S(1)} %fusion.6) | data formatting | bytes 1638400
  (37 shorter events, 0.8 us)
Async XLA Ops:
  0.6 37.7 %copy-start.1 = (f32[16,2048]{1,0:T(8,128)S(1)}, f32[16,2048]{1,0:T(8,128)}, u32[]{:S(2)}) copy-start(f32[16,2048]{1,0:T(8,128)} %param.11) | copy-start | bytes 393220
  0.6 37.6 %copy-start.2 = (bf16[1,50,4096]{2,1,0:T(8,128)(2,1)S(1)}, bf16[1,50,4096]{2,1,0:T(8,128)(2,1)}, u32[]{:S(2)}) copy-start(bf16[1,50,4096]{2,1,0:T(8,128)(2,1)} %param.10) | copy-start | bytes 1228804
  40.6 1.5 %copy-start = (bf16[32,16,2048]{2,1,0:T(8,128)(2,1)}, bf16[32,16,2048]{2,1,0:T(8,128)(2,1)S(1)}, u32[]{:S(2)}) copy-start(bf16[32,16,2048]{2,1,0:T(8,128)(2,1)S(1)} %get-tuple-element.128) | copy-start | bytes 6291460
where the time goes:
time: 79.7 us; the launch traced here: 79.3 us
  blocking collectives  57 us (72%)
  other arithmetic  7.63 us (10%)
  matrix products  6.69 us (8%)
  local copies, waits for them, and re-layouts  5.77 us (7%)
  between operations  2.08 us (3%)
    unnamed x2, blocking collectives  42.9 us
    all_gather x1, blocking collectives, per_device(): everyone = lax.all_gather(particles, 'blk', axis=0, tiled=True)  14.1 us
    unnamed x18, local copies, waits for them, and re-layouts  5.22 us
    dot_general x1, matrix products, accumulate(): lax.dot_general(scaled, shifted, (((0,), (0,)), ((), ())), preferred_elem...  2.57 us
    another operation x2, other arithmetic  2.37 us

commit v1 on v0

--- a/solution.py
+++ b/solution.py
@@ -135,7 +135,20 @@
         ctf_rows = jnp.dot(bin_rows, ctf_table, precision=HIGHEST)
         return (shifted_rows(images, ctf_rows, cosine_table, sine_table), bin_rows)
 
-    everyone = lax.all_gather(particles, "blk", axis=0, tiled=True)
+    def recover_the_node(frame_in, dim_no):
+        nodes = lax.axis_size("blk")
+        ledger = [frame_in]
+        for kk in range(nodes - 1):
+            ledger.append(
+                lax.ppermute(ledger[-1], "blk", [(ii, (ii + 1) % nodes) for ii in range(nodes)])
+            )
+        return jnp.roll(
+            jnp.concatenate(ledger[::-1], dim_no),
+            (lax.axis_index("blk") + 1) * frame_in.shape[dim_no],
+            dim_no,
+        )
+
+    everyone = recover_the_node(particles, dim_no=0)
     gain_all, bins_all, live_all = (
         lax.all_gather(gain_rows, "blk", axis=0, tiled=True),
         lax.all_gather(bin_values, "blk", axis=0, tiled=True),

time: 79.7 us -> 76.9 us (0.965)
  blocking collectives: 57 us -> 39.9 us
  waiting for transfers between devices: 0 us -> 10.5 us
  starting transfers between devices: 0 us -> 3.28 us
  matrix products: 6.69 us -> 7.56 us
    all_gather x1 -> x0, blocking collectives: 14.1 us -> none  [per_device(): everyone = lax.all_gather(particles, 'blk', axis=0, tiled=True)]
    ppermute x0 -> x3, waiting for transfers between devices: none -> 10.5 us  [recover_the_node(): lax.ppermute(ledger[-1], 'blk', [(ii, (ii + 1) % nodes) for ii in range(n...]
    ppermute x0 -> x3, starting transfers between devices: none -> 3.28 us  [recover_the_node(): lax.ppermute(ledger[-1], 'blk', [(ii, (ii + 1) % nodes) for ii in range(n...]
    unnamed x2, blocking collectives: 42.9 us -> 39.9 us
    convert_element_type x1, other arithmetic: 0.06 us -> 1.08 us  [tile_norms(): values = ref_rows.astype(jnp.float32)]
    dot_general x1, matrix products: 0.48 us -> 1.38 us  [tile_norms(): lax.dot_general(ctf_square, power_sum, (((1,), (1,)), ((), ())), precisio...]
    unnamed x18 -> x31, local copies, waits for them, and re-layouts: 5.22 us -> 4.54 us
  transfers between devices with their start and end apart: 0 -> 3, of which waited for: 0 -> 2; matrix products, arithmetic and copies ran while one was open for 0% -> 13% of each run, Pallas kernels for 0% -> 0%
where the time goes in v1:
time: 76.9 us; the launch traced here: 76.6 us
  blocking collectives  39.9 us (52%)
  waiting for transfers between devices  10.5 us (14%)
  other arithmetic  7.88 us (10%)
  matrix products  7.56 us (10%)
  local copies, waits for them, and re-layouts  5.09 us (7%)
  starting transfers between devices  3.28 us (4%)
  between operations  2.21 us (3%)
    unnamed x2, blocking collectives  39.9 us
    ppermute x3, waiting for transfers between devices, recover_the_node(): lax.ppermute(ledger[-1], 'blk', [(ii, (ii + 1) % nodes) for ii in range(n...  10.5 us
    unnamed x31, local copies, waits for them, and re-layouts  4.54 us
    ppermute x3, starting transfers between devices, recover_the_node(): lax.ppermute(ledger[-1], 'blk', [(ii, (ii + 1) % nodes) for ii in range(n...  3.28 us
    dot_general x1, matrix products, accumulate(): lax.dot_general(scaled, shifted, (((0,), (0,)), ((), ())), preferred_elem...  2.57 us
    another operation x2, other arithmetic  2.36 us
  transfers between devices with their start and end apart: 3, of which 2 were waited for; matrix products, arithmetic and copies ran while one was open for 13% of the time, Pallas kernels for 0%

profile of v1, /device:TPU:0, one launch (start us, length us, event | category | flops | bytes accessed | tf_op | source)
XLA Modules:
  0.0 76.6 jit_solution(4754930952773371339)
XLA Ops:
  0.7 3.1 %collective-permute-start = (bf16[8,4096]{1,0:T(8,128)(2,1)}, bf16[8,4096]{1,0:T(8,128)(2,1)S(1)}, u32[]{:S(2)}, u32[]{:S(2)}) collective-permute-start(bf16[8,4096]{1,0:T(8,128)(2,1)} %param.9), channel_id=1, source_target_pairs={{0,4},{4,8},{8,12},{12,0},{1,5},{5,9},{9,13},{13,1},{2,6},{6,10},{... | collective-permute-start | bytes 196616 | tf_op jit(solution)/shard_map/ppermute | solution.py:143
  3.8 0.8 %reduce-window.7 = s32[4,1]{0,1:T(1,128)S(1)} reduce-window(s32[4,1]{0,1:T(1,128)} %bitcast.39, s32[]{:T(128)} %copy.38), window={size=4x1 pad=3_0x0_0}, to_apply=%region_0.1 | reduce-window | flops 12 | bytes 36 | tf_op jit(solution)/shard_map/reduce-window.2
  4.6 0.7 bitcast_subtract_fusion
  5.3 0.1 mul.363
  5.5 1.1 %bitcast_convert_fusion = f32[50,4096]{1,0:T(8,128)S(1)} fusion(bf16[1,50,4096]{2,1,0:T(8,128)(2,1)} %param.10), kind=kLoop, calls=%fused_computation.23 | loop fusion | flops 204800 | bytes 1228800 | tf_op jit(solution)/shard_map/convert_element_type | solution.py:69
  6.6 1.2 %dynamic-slice = u32[1]{0:T(128)} dynamic-slice(u32[32]{0:T(128)} %constant.113, u32[]{:T(128)S(6)} %add.123), dynamic_slice_sizes={1} | dynamic-slice | bytes 12
  8.5 0.7 select_reduce_fusion
  9.2 0.2 dynamic-update-slice.4
  9.5 0.7 convert_dynamic-update-slice_fusion
  10.2 0.2 dynamic-update-slice
  10.4 10.4 %all-reduce.6 = (f32[32]{0:T(128)S(1)}, f32[32]{0:T(128)S(1)}, f32[32]{0:T(128)S(1)}) all-reduce(f32[32]{0:T(128)S(1)} %convert_dynamic-update-slice_fusion, f32[32]{0:T(128)S(1)} %dynamic-update-slice.4, f32[32]{0:T(128)S(1)} %dynamic-update-slice), channel_id=1, replica_groups=mesh['groups'=2,'blk'=4,'cls'=4] {'blk'}, use_global_device_ids=true, to_apply=%add.1 | all-reduce | flops 96 | bytes 768
  20.8 1.2 %fusion.22 = f32[32,2048]{1,0:T(8,128)S(1)} fusion(f32[16,2048]{1,0:T(8,128)} %param.11, f32[32]{0:T(128)S(1)} %get-tuple-element.122), kind=kOutput, calls=%fused_computation.48 | convolution fusion | flops 12583424 | bytes 393344 | tf_op jit(solution)/shard_map/while/body/eval_jaxpr/dot_general | solution.py:135
  22.0 1.4 %fusion.11 = f32[16,50]{1,0:T(8,128)S(1)} fusion(f32[50,4096]{1,0:T(8,128)S(1)} %bitcast_convert_fusion, f32[16,2048]{1,0:T(8,128)} %param.11), kind=kOutput, calls=%fused_computation.20 | convolution fusion | flops 20000768 | bytes 953472 | tf_op jit(solution)/shard_map/dot_general | solution.py:74
  23.4 0.6 fusion.15
  24.0 0.2 collective-permute-start.1
  24.2 0.2 convolution_multiply_fusion
  24.4 0.6 dynamic-slice.2
  25.6 4.4 %collective-permute-done.1 = bf16[8,4096]{1,0:T(8,128)(2,1)S(1)} collective-permute-done((bf16[8,4096]{1,0:T(8,128)(2,1)S(1)}, bf16[8,4096]{1,0:T(8,128)(2,1)S(1)}, u32[]{:S(2)}, u32[]{:S(2)}) %collective-permute-start.1) | collective-permute-done | bytes 65568 | tf_op jit(solution)/shard_map/ppermute | solution.py:143
  30.1 6.1 %collective-permute-done.2 = bf16[8,4096]{1,0:T(8,128)(2,1)S(1)} collective-permute-done((bf16[8,4096]{1,0:T(8,128)(2,1)S(1)}, bf16[8,4096]{1,0:T(8,128)(2,1)S(1)}, u32[]{:S(2)}, u32[]{:S(2)}) %collective-permute-start.2) | collective-permute-done | bytes 65568 | tf_op jit(solution)/shard_map/ppermute | solution.py:143
  36.3 1.5 %multiply_convert_fusion.1 = (bf16[32,16,2048]{2,1,0:T(8,128)(2,1)S(1)}, bf16[32,16,2048]{2,1,0:T(8,128)(2,1)S(1)}) fusion(f32[32,2048]{1,0:T(8,128)S(1)} %fusion.22, f32[16,2048]{1,0:T(8,128)S(1)} %get-tuple-element.132, f32[32,2048]{1,0:T(8,128)S(1)} %get-tuple-element.130, f32[16,2048]{1,0:T(8,128)S(1)} %get-tuple-element.131, ...), kind=kLoop, calls=%fused_computation.12 | loop fusion | flops 10485760 | bytes 5242880 | tf_op jit(solution)/shard_map/convert
  37.9 1.4 %fusion.40 = (f32[32]{0:T(128)S(1)}, f32[32,16,50]{2,1,0:T(8,128)S(1)}) fusion(f32[32,50]{1,0:T(8,128)S(1)} %convolution_multiply_fusion, bf16[1,50,4096]{2,1,0:T(8,128)(2,1)S(1)} %copy-done.2, bf16[32,16,2048]{2,1,0:T(8,128)(2,1)S(1)} %get-tuple-element.128, bf16[32,16,2048]{2,1,0:T(8,128)(2,1)S(1)} %get-tuple-element.127, f32[32]{0:T(128)S(1)} %get-tuple-element.124), kind=kOutput, calls=%fused_computation.79 | convolution fusion | flops 218180576 | bytes 4712960 | tf_op jit(solution)/shard_map/while/body/eval_jaxpr/dot_general | solution.py:79
  39.3 0.5 exponential_reduce_fusion
  39.8 0.2 dynamic-update-slice.2
  40.1 0.2 dynamic-update-slice.3
  40.3 29.5 %all-reduce.5 = (f32[512]{0:T(512)S(1)}, f32[512]{0:T(512)S(1)}) all-reduce(f32[512]{0:T(512)S(1)} %dynamic-update-slice.2, f32[512]{0:T(512)S(1)} %dynamic-update-slice.3), channel_id=2, replica_groups=mesh['groups'=2,'blk'=4,'cls'=4] {'blk','cls'}, use_global_device_ids=true, to_apply=%add.2 | all-reduce | flops 1024 | bytes 8192
  70.1 0.6 while.2
  70.7 0.6 compare_select_fusion
  71.3 0.2 fusion.38
  71.4 0.3 fusion.20
  71.7 0.5 fusion.17
  72.3 2.6 %fusion.6 = f32[1,50,4096]{2,1,0:T(8,128)S(1)} fusion(bf16[32,16,2048]{2,1,0:T(8,128)(2,1)} %copy-done, bf16[32,16,2048]{2,1,0:T(8,128)(2,1)S(1)} %get-tuple-element.127, f32[50,2048]{1,0:T(8,128)S(1)} %fusion.17, f32[4096]{0:T(1024)S(1)} %pad_maximum_fusion.7, f32[32]{0:T(128)S(1)} %get-tuple-element.124, f32[32,16,50]{2,1,0:T(8,128)S(1)} %get-tuple-element.136, ...), kind=kOutput, calls=%fused_computation.9 | convolution fusion | flops 218846208 | bytes 5542400 | tf_op jit(solution)/shard_map/while/body/eval_jaxpr/dot_general | solution.py:105
  74.8 1.7 %copy.14 = f32[1,50,4096]{2,0,1:T(1,128)} copy(f32[1,50,4096]{2,1,0:T(8,128)S(1)} %fusion.6) | data formatting | bytes 1638400
  (56 shorter events, 1.0 us)
Async XLA Ops:
  0.6 23.8 %copy-start.5 = (u32[32]{0:T(128)S(1)}, u32[32]{0:T(128)}, u32[]{:S(2)}) copy-start(u32[32]{0:T(128)} %constant.123) | copy-start | bytes 388
  0.6 35.5 %copy-start.3 = (bf16[8,4096]{1,0:T(8,128)(2,1)S(1)}, bf16[8,4096]{1,0:T(8,128)(2,1)}, u32[]{:S(2)}) copy-start(bf16[8,4096]{1,0:T(8,128)(2,1)} %param.9) | copy-start | bytes 196612
  0.7 29.4 %copy-start.4 = (f32[2048]{0:T(1024)S(1)}, f32[2048]{0:T(1024)}, u32[]{:S(2)}) copy-start(f32[2048]{0:T(1024)} %param.12) | copy-start | bytes 24580
  0.7 23.3 %collective-permute-start = (bf16[8,4096]{1,0:T(8,128)(2,1)}, bf16[8,4096]{1,0:T(8,128)(2,1)S(1)}, u32[]{:S(2)}, u32[]{:S(2)}) collective-permute-start(bf16[8,4096]{1,0:T(8,128)(2,1)} %param.9), channel_id=1, source_target_pairs={{0,4},{4,8},{8,12},{12,0},{1,5},{5,9},{9,13},{13,1},{2,6},{6,10},{... | collective-permute-start | bytes 196616 | tf_op jit(solution)/shard_map/ppermute | solution.py:143
  24.0 6.1 %collective-permute-start.1 = (bf16[8,4096]{1,0:T(8,128)(2,1)S(1)}, bf16[8,4096]{1,0:T(8,128)(2,1)S(1)}, u32[]{:S(2)}, u32[]{:S(2)}) collective-permute-start(bf16[8,4096]{1,0:T(8,128)(2,1)S(1)} %collective-permute-done), channel_id=1, source_target_pairs={{0,4},{4,8},{8,12},{12,0},{1,5},{5,9},{9,13},{13,1},{2,6},{6,10},{... | collective-permute-start | bytes 196616 | tf_op jit(solution)/shard_map/ppermute | solution.py:143
  30.1 6.1 %collective-permute-start.2 = (bf16[8,4096]{1,0:T(8,128)(2,1)S(1)}, bf16[8,4096]{1,0:T(8,128)(2,1)S(1)}, u32[]{:S(2)}, u32[]{:S(2)}) collective-permute-start(bf16[8,4096]{1,0:T(8,128)(2,1)S(1)} %collective-permute-done.1), channel_id=1, source_target_pairs={{0,4},{4,8},{8,12},{12,0},{1,5},{5,9},{9,13},{13,1},{2,6},{6,10},{... | collective-permute-start | bytes 196616 | tf_op jit(solution)/shard_map/ppermute | solution.py:143
  36.3 1.6 %copy-start.2 = (bf16[1,50,4096]{2,1,0:T(8,128)(2,1)S(1)}, bf16[1,50,4096]{2,1,0:T(8,128)(2,1)}, u32[]{:S(2)}) copy-start(bf16[1,50,4096]{2,1,0:T(8,128)(2,1)} %param.10) | copy-start | bytes 1228804
  37.9 1.5 %copy-start = (bf16[32,16,2048]{2,1,0:T(8,128)(2,1)}, bf16[32,16,2048]{2,1,0:T(8,128)(2,1)S(1)}, u32[]{:S(2)}) copy-start(bf16[32,16,2048]{2,1,0:T(8,128)(2,1)S(1)} %get-tuple-element.128) | copy-start | bytes 6291460
  37.9 33.9 %copy-start.1 = (f32[16,2048]{1,0:T(8,128)S(1)}, f32[16,2048]{1,0:T(8,128)}, u32[]{:S(2)}) copy-start(f32[16,2048]{1,0:T(8,128)} %param.11) | copy-start | bytes 393220
